TPU v7x, 512 devices: a whole 4x4x16 slice. The times are simulated.
512 devices in a mesh: req: 128 (over z, y, core), tp: 4 (over x).
Axes of the slice: x: 4, y: 4, z: 16, core: 2. Of those that a mesh axis runs over, the one named last changes fastest.
Arguments:
- states: bfloat16 [32768, 3072], P('req', 'tp'), may hold values from -12 to 12
- query_weight: bfloat16 [3072, 1536], P(None, 'tp'), may hold values from -0.75 to 0.75
- key_value_weight: bfloat16 [3072, 512], P(None, 'tp'), may hold values from -0.75 to 0.75
- lengths: int32 [128], P('req'), may hold values from 1 to 256, 16384 in all
- adapter_ids: int32 [128], P('req'), may hold values from 0 to 63, as said below
- adapter_slot: int32 [64], replicated, may hold values from 0 to 127, as said below
- down_store: bfloat16 [128, 3072, 32], P('req', 'tp'), may hold values from -0.109375 to 0.109375
- query_up_store: bfloat16 [128, 16, 1536], P('req', None, 'tp'), may hold values from -1.5 to 1.5
- key_value_store: bfloat16 [128, 16, 512], P('req', None, 'tp'), may hold values from -1.5 to 1.5
Outputs:
- context: bfloat16 [32768, 1536], P('req', 'tp')
Inputs may be any that keep to these rules, and one draw needn't show every extreme that they name: `adapter_ids`: exactly 16 distinct adapters are named among all 128 requests. `adapter_slot`: distinct adapters have distinct rows.
All inputs are finite; a program needn't handle non-finite values. No bound on the sum of `lengths` on one device may be relied on, other than what follows from the above.
Results may differ from a plain program's by a relative error of at most 0.0072.
Values may be sent and summed in bfloat16 or wider, within the bound.
No kernel may reach another device: no remote copies, remote signals or barrier semaphores. Data moves between devices by JAX's collectives and lax.ppermute only.
A program may use at most 64 MiB of HBM per device.

v0:
```python
import math
import jax
import jax.numpy as jnp
from jax import lax
from jax.sharding import PartitionSpec as P

HEADS = 12
HEAD_DIM = 128
adapter_scale = 0.5
rope_base = 100000000000.0


def rotate(field):
    half = field.shape[-1] // 2
    count = field.shape[-3]
    position = jnp.arange(count).astype(jnp.float32)
    inverse = rope_base ** (-(jnp.arange(half).astype(jnp.float32) * 2.0) / field.shape[-1])
    angle = position[:, None] * inverse[None, :]
    cosine = jnp.cos(angle)[:, None, :]
    sine = jnp.sin(angle)[:, None, :]
    first_half = field[..., :half]
    second_half = field[..., half:]
    return jnp.concatenate(
        [first_half * cosine - second_half * sine, second_half * cosine + first_half * sine],
        axis=-1,
    )


def lookup_slots(wanted, adapter_slot):
    table = jnp.arange(adapter_slot.shape[0], dtype=jnp.int32)
    matches = wanted[:, None] == table[None, :]
    return jnp.sum(jnp.where(matches, adapter_slot[None, :], 0), axis=1)


def local(
    states,
    query_weight,
    key_value_weight,
    lengths,
    adapter_ids,
    adapter_slot,
    down_store,
    query_up_store,
    key_value_store,
):
    tp_index = lax.axis_index("tp")
    req_dev = lengths.shape[0]
    rows_total = states.shape[0]
    slot_len = rows_total // req_dev
    q_cols = query_weight.shape[1]
    kv_cols = key_value_weight.shape[1]
    heads_here = q_cols // HEAD_DIM
    pooled = (
        lax.all_gather(down_store, "req", axis=0, tiled=True),
        lax.all_gather(query_up_store, "req", axis=0, tiled=True),
        lax.all_gather(key_value_store, "req", axis=0, tiled=True),
    )
    own_slots = lookup_slots(adapter_ids, adapter_slot)
    adapter_down, adapter_query, adapter_pair = (
        jnp.take(member, own_slots, axis=0) for member in pooled
    )
    full_down = lax.all_gather(adapter_down, "tp", axis=1, tiled=True)
    piece = lax.all_gather(states, "tp", axis=1, tiled=True)
    width = piece.shape[1]
    grouped = piece.reshape(req_dev, slot_len, width)
    query_total = jnp.dot(piece, query_weight, preferred_element_type=jnp.float32)
    key_value_sum = jnp.dot(piece, key_value_weight, preferred_element_type=jnp.float32)
    rank_sum = jnp.einsum("rsd,rdk->rsk", grouped, full_down, preferred_element_type=jnp.float32)
    rank_mid = rank_sum.astype(jnp.bfloat16)
    rank_cols = rank_mid.shape[2] // 2
    query_addition = jnp.einsum(
        "rsk,rkc->rsc",
        rank_mid[:, :, :rank_cols],
        adapter_query,
        preferred_element_type=jnp.float32,
    ).reshape(rows_total, q_cols)
    key_value_extra = jnp.einsum(
        "rsk,rkc->rsc", rank_mid[:, :, rank_cols:], adapter_pair, preferred_element_type=jnp.float32
    ).reshape(rows_total, kv_cols)
    query_plain = query_total + adapter_scale * query_addition
    key_value_own = (key_value_sum + adapter_scale * key_value_extra).astype(jnp.bfloat16)
    pair_all = lax.all_gather(key_value_own, "tp", axis=1, tiled=True)
    key_width = pair_all.shape[1] // 2
    kv_heads = key_width // HEAD_DIM
    group = HEADS // kv_heads
    kv_index = tp_index * heads_here // group
    key_block = lax.dynamic_slice_in_dim(pair_all, kv_index * HEAD_DIM, HEAD_DIM, 1)
    value_block = lax.dynamic_slice_in_dim(pair_all, key_width + kv_index * HEAD_DIM, HEAD_DIM, 1)
    queries = rotate(query_plain.reshape(req_dev, slot_len, heads_here, HEAD_DIM)).astype(
        jnp.bfloat16
    )
    keys_one = rotate(key_block.astype(jnp.float32).reshape(req_dev, slot_len, 1, HEAD_DIM)).astype(
        jnp.bfloat16
    )[:, :, 0, :]
    values_one = value_block.reshape(req_dev, slot_len, HEAD_DIM)
    scale = 1.0 / math.sqrt(HEAD_DIM)
    scores = (
        jnp.einsum("rqhd,rkd->rhqk", queries, keys_one, preferred_element_type=jnp.float32) * scale
    )
    position = jnp.arange(slot_len, dtype=jnp.int32)
    allowed = (position[None, None, :] <= position[None, :, None]) & (
        position[None, None, :] < lengths[:, None, None]
    )
    scores = jnp.where(allowed[:, None, :, :], scores, -jnp.inf)
    highest = jnp.max(scores, axis=-1, keepdims=True)
    expo = jnp.exp(scores - highest)
    weights = (expo / jnp.sum(expo, axis=-1, keepdims=True)).astype(jnp.bfloat16)
    context = jnp.einsum("rhqk,rkd->rqhd", weights, values_one, preferred_element_type=jnp.float32)
    live_rows = position[None, :] < lengths[:, None]
    context = jnp.where(live_rows[:, :, None, None], context, 0.0)
    return context.reshape(rows_total, q_cols).astype(jnp.bfloat16)


def solution(mesh):
    return jax.shard_map(
        local,
        mesh=mesh,
        in_specs=(
            P("req", "tp"),
            P(None, "tp"),
            P(None, "tp"),
            P("req"),
            P("req"),
            P(),
            P("req", "tp", None),
            P("req", None, "tp"),
            P("req", None, "tp"),
        ),
        out_specs=P("req", "tp"),
        check_vma=False,
    )
```

profile of v0, /device:TPU:2, one launch (start us, length us, event | category | flops | bytes accessed | tf_op | source)
XLA Modules:
  0.0 358.5 jit_solution(2716103049818812552)
XLA Ops:
  6.5 0.0 copy-start
  6.5 0.0 all-gather.4.cloned.1.call-start
  6.5 0.7 all-gather.4.cloned.1.call-update
  7.3 0.0 all-gather.6.cloned.1.call-start
  7.3 0.7 all-gather.6.cloned.1.call-update
  8.0 0.0 all-gather.8.cloned.1.call-start
  8.1 0.7 all-gather.8.cloned.1.call-update
  9.4 1.3 fusion.39
  13.3 0.0 copy-start.4
  13.4 0.0 copy-start.6
  13.4 0.0 copy-start.2
  13.4 96.3 %all_gather.21 = bf16[128,16,128]{2,1,0:T(8,128)(2,1)} all-gather(bf16[1,16,128]{2,1,0:T(8,128)(2,1)} %param.17), channel_id=1, replica_groups=mesh['req'=128,'tp'=4] {'req'}, dimensions={0}, use_global_device_ids=true | all-gather | bytes 528384 | tf_op jit(solution)/shard_map/all_gather | solution.py:56
  109.7 0.0 copy-done.6
  109.7 0.1 fusion.9
  109.8 0.0 copy-done.4
  109.8 0.0 copy-done.2
  109.8 1.2 multiply_cosine_fusion
  111.0 0.0 all-gather.4.cloned.1.call-done
  111.0 0.0 copy-done
  111.0 2.4 fusion.45
  113.4 82.7 %all-gather.6.cloned.1.call-done = bf16[128,768,32]{1,2,0:T(8,128)(2,1)} async-done(((bf16[1,768,32]{1,2,0:T(8,128)(2,1)}), bf16[128,768,32]{1,2,0:T(8,128)(2,1)}) %all-gather.6.cloned.1.call-update) | async-done | bytes 6291472 | tf_op jit(solution)/shard_map/all_gather | solution.py:54
  196.1 0.8 dynamic-slice_select_fusion
  196.9 12.4 %all_gather.20 = bf16[1,3072,32]{1,2,0:T(8,128)(2,1)S(1)} all-gather(bf16[1,768,32]{1,2,0:T(8,128)(2,1)S(1)} %dynamic-slice_select_fusion), channel_id=1, replica_groups=mesh['req'=128,'tp'=4] {'tp'}, dimensions={1}, use_global_device_ids=true | all-gather | bytes 245760 | tf_op jit(solution)/shard_map/all_gather | solution.py:62
  209.3 2.0 fusion.6
  211.2 121.7 %all-gather.8.cloned.1.call-done = bf16[128,16,384]{2,1,0:T(8,128)(2,1)} async-done(((bf16[1,16,384]{2,1,0:T(8,128)(2,1)}), bf16[128,16,384]{2,1,0:T(8,128)(2,1)}) %all-gather.8.cloned.1.call-update) | async-done | bytes 1572880 | tf_op jit(solution)/shard_map/all_gather | solution.py:55
  332.9 1.0 fusion.2
  333.9 0.2 copy.21
  334.1 0.2 copy.30
  334.3 0.2 copy.31
  334.4 0.9 convolution_multiply_fusion.2
  335.3 0.0 copy-start.3
  335.3 0.0 copy-start.5
  335.4 0.0 copy-start.1
  335.4 2.2 fusion.5
  337.6 12.0 %all_gather.22 = bf16[256,512]{1,0:T(8,128)(2,1)S(1)} all-gather(bf16[256,128]{1,0:T(8,128)(2,1)S(1)} %fusion.5), channel_id=1, replica_groups=mesh['req'=128,'tp'=4] {'tp'}, dimensions={1}, use_global_device_ids=true | all-gather | bytes 327680 | tf_op jit(solution)/shard_map/all_gather | solution.py:82
  349.6 0.0 copy-done.3
  349.6 0.0 copy-done.5
  349.6 0.6 fusion.29
  350.2 0.0 copy-done.1
  350.2 0.0 copy-start.7
  350.2 0.1 fusion.10
  350.4 0.4 fusion.44
  350.7 0.1 fusion.7
  350.9 0.0 copy-done.7
  350.9 0.3 fusion.4
  351.2 0.8 copy.26
  (5 shorter events, 0.1 us)
Async XLA Ops:
  6.5 104.5 %copy-start = (bf16[3072,384]{1,0:T(8,128)(2,1)S(1)}, bf16[3072,384]{1,0:T(8,128)(2,1)}, u32[]{:S(2)}) copy-start(bf16[3072,384]{1,0:T(8,128)(2,1)} %param.10) | copy-start | bytes 7077892
  6.5 104.5 %all-gather.4.cloned.1.call-start = ((), (), s32[]{:S(2)}) async-start(), calls=%async_computation | async-start | bytes 1966080 | tf_op jit(solution)/shard_map/all_gather | solution.py:63
  7.3 188.8 %all-gather.6.cloned.1.call-start = ((), (), s32[]{:S(2)}) async-start(), calls=%async_computation.1 | async-start | bytes 6340608 | tf_op jit(solution)/shard_map/all_gather | solution.py:54
  8.0 324.9 %all-gather.8.cloned.1.call-start = ((), (), s32[]{:S(2)}) async-start(), calls=%async_computation.2 | async-start | bytes 1585152 | tf_op jit(solution)/shard_map/all_gather | solution.py:55
  13.3 96.5 %copy-start.4 = (f32[64]{0:T(128)}, f32[64]{0:T(128)S(1)}, u32[]{:S(2)}) copy-start(f32[64]{0:T(128)S(1)} %multiply_power_fusion) | copy-start | bytes 772
  13.4 96.3 %copy-start.6 = (pred[256]{0:T(512)(128)(4,1)}, pred[256]{0:T(512)(128)(4,1)S(1)}, u32[]{:S(2)}) copy-start(pred[256]{0:T(512)(128)(4,1)S(1)} %iota_compare_fusion.1) | copy-start | bytes 772
  13.4 96.4 %copy-start.2 = (f32[256]{0:T(256)}, f32[256]{0:T(256)S(1)}, u32[]{:S(2)}) copy-start(f32[256]{0:T(256)S(1)} %iota_convert_fusion) | copy-start | bytes 3076
  335.3 14.3 %copy-start.3 = (f32[256]{0:T(256)S(1)}, f32[256]{0:T(256)}, u32[]{:S(2)}) copy-start(f32[256]{0:T(256)} %copy-done.2) | copy-start | bytes 3076
  335.3 14.3 %copy-start.5 = (f32[64]{0:T(128)S(1)}, f32[64]{0:T(128)}, u32[]{:S(2)}) copy-start(f32[64]{0:T(128)} %copy-done.4) | copy-start | bytes 772
  335.4 14.9 %copy-start.1 = (f32[256,64]{1,0:T(8,128)S(1)}, f32[256,64]{1,0:T(8,128)}, u32[]{:S(2)}) copy-start(f32[256,64]{1,0:T(8,128)} %get-tuple-element.45) | copy-start | bytes 196612
  350.2 0.7 copy-start.7
Sparse Core Ops, SparseCore 0:
  9.5 37.5 all-gather.3
  50.2 145.7 all-gather.5
  199.1 133.7 all-gather.7
where the time goes:
time: 359 us
  waiting for transfers between devices  206 us (57%)
  blocking collectives  121 us (34%)
  between operations  16.5 us (5%)
  matrix products  9.02 us (3%)
  other arithmetic  4.29 us (1%)
    all_gather x1, waiting for transfers between devices, local(): lax.all_gather(query_up_store, 'req', axis=0, tiled=True)  122 us
    all_gather x1, blocking collectives, local(): lax.all_gather(key_value_store, 'req', axis=0, tiled=True)  96.3 us
    all_gather x1, waiting for transfers between devices, local(): lax.all_gather(down_store, 'req', axis=0, tiled=True)  82.7 us
    all_gather x1, blocking collectives, local(): full_down = lax.all_gather(adapter_down, 'tp', axis=1, tiled=True)  12.4 us
    all_gather x1, blocking collectives, local(): pair_all = lax.all_gather(key_value_own, 'tp', axis=1, tiled=True)  12 us
  transfers between devices with their start and end apart: 3, of which 2 were waited for; matrix products, arithmetic and copies ran while one was open for 2% of the time, Pallas kernels for 0%

commit v1 on v0

--- a/solution.py
+++ b/solution.py
@@ -8,6 +8,20 @@
 HEAD_DIM = 128
 adapter_scale = 0.5
 rope_base = 100000000000.0
+
+
+def step_on_gates(tile_in, dim_i):
+    nd = lax.axis_size("tp")
+    windows = [tile_in]
+    for at in tuple(range(nd - 1)):
+        windows.append(
+            lax.ppermute(windows[-1], axis_name="tp", perm=[(m, (m + 1) % nd) for m in range(nd)])
+        )
+    return jnp.roll(
+        jnp.concatenate(windows[::-1], axis=dim_i),
+        (lax.axis_index("tp") + 1) * tile_in.shape[dim_i],
+        axis=dim_i,
+    )
 
 
 def rotate(field):
@@ -79,7 +93,7 @@
     ).reshape(rows_total, kv_cols)
     query_plain = query_total + adapter_scale * query_addition
     key_value_own = (key_value_sum + adapter_scale * key_value_extra).astype(jnp.bfloat16)
-    pair_all = lax.all_gather(key_value_own, "tp", axis=1, tiled=True)
+    pair_all = step_on_gates(key_value_own, 1)
     key_width = pair_all.shape[1] // 2
     kv_heads = key_width // HEAD_DIM
     group = HEADS // kv_heads

time: 359 us -> 361 us (level)
  the two profiles are of different devices: /device:TPU:2 before, /device:TPU:1 now
where the time goes in v1:
time: 361 us
  waiting for transfers between devices  210 us (58%)
  blocking collectives  108 us (30%)
  between operations  16.5 us (5%)
  matrix products  8.68 us (2%)
  starting transfers between devices  7.33 us (2%)
  other arithmetic  5.65 us (2%)
  local copies, waits for them, and re-layouts  4.76 us (1%)
    all_gather x1, waiting for transfers between devices, local(): lax.all_gather(query_up_store, 'req', axis=0, tiled=True)  120 us
    all_gather x1, blocking collectives, local(): lax.all_gather(key_value_store, 'req', axis=0, tiled=True)  97.6 us
    all_gather x1, waiting for transfers between devices, local(): lax.all_gather(down_store, 'req', axis=0, tiled=True)  81.3 us
    all_gather x1, blocking collectives, local(): full_down = lax.all_gather(adapter_down, 'tp', axis=1, tiled=True)  10.1 us
    ppermute x3, starting transfers between devices, step_on_gates(): lax.ppermute(windows[-1], axis_name='tp', perm=[(m, (m + 1) % nd) for m i...  7.25 us
  transfers between devices with their start and end apart: 6, of which 4 were waited for; matrix products, arithmetic and copies ran while one was open for 4% of the time, Pallas kernels for 0%

profile of v1, /device:TPU:1, one launch (start us, length us, event | category | flops | bytes accessed | tf_op | source)
XLA Modules:
  0.0 360.6 jit_solution(9821971737456508959)
XLA Ops:
  6.5 0.0 copy-start
  6.5 0.0 all-gather.4.cloned.1.call-start
  6.5 0.7 all-gather.4.cloned.1.call-update
  7.3 0.0 all-gather.6.cloned.1.call-start
  7.3 0.7 all-gather.6.cloned.1.call-update
  8.0 0.0 all-gather.8.cloned.1.call-start
  8.1 0.7 all-gather.8.cloned.1.call-update
  9.4 1.3 fusion.39
  13.3 97.6 %all_gather.18 = bf16[128,16,128]{2,1,0:T(8,128)(2,1)} all-gather(bf16[1,16,128]{2,1,0:T(8,128)(2,1)} %param.17), channel_id=1, replica_groups=mesh['req'=128,'tp'=4] {'req'}, dimensions={0}, use_global_device_ids=true | all-gather | bytes 528384 | tf_op jit(solution)/shard_map/all_gather | solution.py:70
  110.9 0.7 fusion.9
  111.6 1.2 multiply_cosine_fusion
  112.8 0.0 all-gather.4.cloned.1.call-done
  112.8 0.0 copy-done
  112.8 0.0 copy-start.2
  112.8 3.2 fusion.45
  116.0 81.3 %all-gather.6.cloned.1.call-done = bf16[128,768,32]{1,2,0:T(8,128)(2,1)} async-done(((bf16[1,768,32]{1,2,0:T(8,128)(2,1)}), bf16[128,768,32]{1,2,0:T(8,128)(2,1)}) %all-gather.6.cloned.1.call-update) | async-done | bytes 6291472 | tf_op jit(solution)/shard_map/all_gather | solution.py:68
  197.3 0.0 copy-start.1
  197.3 0.9 dynamic-slice_select_fusion
  198.3 10.1 %all_gather.17 = bf16[1,3072,32]{1,2,0:T(8,128)(2,1)S(1)} all-gather(bf16[1,768,32]{1,2,0:T(8,128)(2,1)S(1)} %dynamic-slice_select_fusion), channel_id=1, replica_groups=mesh['req'=128,'tp'=4] {'tp'}, dimensions={1}, use_global_device_ids=true | all-gather | bytes 245760 | tf_op jit(solution)/shard_map/all_gather | solution.py:76
  208.4 2.0 fusion.6
  210.3 0.9 convolution_multiply_fusion.2
  211.2 0.0 copy-done.2
  211.3 0.0 copy-done.1
  211.3 0.7 fusion.5
  211.9 2.3 collective-permute-start
  214.2 120.0 %all-gather.8.cloned.1.call-done = bf16[128,16,384]{2,1,0:T(8,128)(2,1)} async-done(((bf16[1,16,384]{2,1,0:T(8,128)(2,1)}), bf16[128,16,384]{2,1,0:T(8,128)(2,1)}) %all-gather.8.cloned.1.call-update) | async-done | bytes 1572880 | tf_op jit(solution)/shard_map/all_gather | solution.py:69
  334.2 1.3 fusion.2
  335.5 0.2 copy.21
  335.7 0.0 collective-permute-done
  335.7 3.1 collective-permute-start.1
  338.8 0.2 copy.30
  339.0 0.2 copy.31
  339.2 0.0 copy-start.3
  339.2 3.0 collective-permute-done.1
  342.2 1.9 collective-permute-start.2
  344.1 1.0 fusion.10
  345.2 3.5 collective-permute-done.2
  348.6 0.8 constant_dynamic-update-slice_fusion.6
  349.5 0.8 constant_dynamic-update-slice_fusion.5
  350.4 0.8 constant_dynamic-update-slice_fusion.2
  351.2 0.8 constant_dynamic-update-slice_fusion.1
  352.1 0.3 fusion.29
  352.4 0.0 copy-done.3
  352.4 0.4 fusion.44
  352.8 0.1 fusion.7
  353.0 0.3 fusion.4
  353.2 0.8 copy.26
  (9 shorter events, 0.1 us)
Async XLA Ops:
  6.5 106.3 %copy-start = (bf16[3072,384]{1,0:T(8,128)(2,1)S(1)}, bf16[3072,384]{1,0:T(8,128)(2,1)}, u32[]{:S(2)}) copy-start(bf16[3072,384]{1,0:T(8,128)(2,1)} %param.10) | copy-start | bytes 7077892
  6.5 106.3 %all-gather.4.cloned.1.call-start = ((), (), s32[]{:S(2)}) async-start(), calls=%async_computation | async-start | bytes 1966080 | tf_op jit(solution)/shard_map/all_gather | solution.py:77
  7.3 190.1 %all-gather.6.cloned.1.call-start = ((), (), s32[]{:S(2)}) async-start(), calls=%async_computation.1 | async-start | bytes 6340608 | tf_op jit(solution)/shard_map/all_gather | solution.py:68
  8.0 326.2 %all-gather.8.cloned.1.call-start = ((), (), s32[]{:S(2)}) async-start(), calls=%async_computation.2 | async-start | bytes 1585152 | tf_op jit(solution)/shard_map/all_gather | solution.py:69
  112.8 98.4 %copy-start.2 = (bf16[3072,128]{1,0:T(8,128)(2,1)S(1)}, bf16[3072,128]{1,0:T(8,128)(2,1)}, u32[]{:S(2)}) copy-start(bf16[3072,128]{1,0:T(8,128)(2,1)} %param.11) | copy-start | bytes 2359300
  197.3 13.9 %copy-start.1 = (bf16[256,3072]{1,0:T(8,128)(2,1)S(1)}, bf16[256,3072]{1,0:T(8,128)(2,1)}, u32[]{:S(2)}) copy-start(bf16[256,3072]{1,0:T(8,128)(2,1)} %all-gather.4.cloned.1.call-done) | copy-start | bytes 4718596
  211.9 123.7 %collective-permute-start = (bf16[256,128]{0,1:T(8,128)(2,1)S(1)}, bf16[256,128]{0,1:T(8,128)(2,1)}, u32[]{:S(2)}, u32[]{:S(2)}) collective-permute-start(bf16[256,128]{0,1:T(8,128)(2,1)S(1)} %fusion.5), channel_id=1, source_target_pairs={{0,1},{1,2},{2,3},{3,0},{4,5},{5,6},{6,7},{7,4},{8,9},{9,10},{10,1... | collective-permute-start | bytes 196616 | tf_op jit(solution)/shard_map/ppermute | solution.py:18
  335.7 6.5 %collective-permute-start.1 = (bf16[256,128]{0,1:T(8,128)(2,1)}, bf16[256,128]{0,1:T(8,128)(2,1)}, u32[]{:S(2)}, u32[]{:S(2)}) collective-permute-start(bf16[256,128]{0,1:T(8,128)(2,1)} %collective-permute-done), channel_id=1, source_target_pairs={{0,1},{1,2},{2,3},{3,0},{4,5},{5,6},{6,7},{7,4},{8,9},{9,10},{10,1... | collective-permute-start | bytes 196616 | tf_op jit(solution)/shard_map/ppermute | solution.py:18
  339.2 13.3 %copy-start.3 = (pred[256,256]{0,1:T(8,128)(4,1)S(1)}, pred[256,256]{0,1:T(8,128)(4,1)}, u32[]{:S(2)}) copy-start(pred[256,256]{0,1:T(8,128)(4,1)} %fusion.9) | copy-start | bytes 196612
  342.2 6.4 %collective-permute-start.2 = (bf16[256,128]{0,1:T(8,128)(2,1)}, bf16[256,128]{0,1:T(8,128)(2,1)S(1)}, u32[]{:S(2)}, u32[]{:S(2)}) collective-permute-start(bf16[256,128]{0,1:T(8,128)(2,1)} %collective-permute-done.1), channel_id=1, source_target_pairs={{0,1},{1,2},{2,3},{3,0},{4,5},{5,6},{6,7},{7,4},{8,9},{9,10},{10,1... | collective-permute-start | bytes 196616 | tf_op jit(solution)/shard_map/ppermute | solution.py:18
Sparse Core Ops, SparseCore 0:
  9.5 39.4 all-gather.3
  52.1 145.1 all-gather.5
  200.4 133.7 all-gather.7
